TPU v7x, 32 devices: a whole 2x2x4 slice. The times are simulated.
32 devices in a mesh: dp: 4 (over z), fsdp: 2 (over x), rows: 4 (over y, core).
Axes of the slice: x: 2, y: 2, z: 4, core: 2. Of those that a mesh axis runs over, the one named last changes fastest.
Arguments:
- feature_maps: bfloat16 [8, 16, 32, 1536], P(('dp', 'fsdp'), 'rows'), may hold values from -30 to 30
- dw_kernel: float32 [7, 7, 1536], replicated, may hold values from -0.875 to 0.875
- norm_gain: float32 [1536], replicated, may hold values from 0.5 to 1.5
- w_up: bfloat16 [1536, 6144], P(('dp', 'rows'), 'fsdp'), may hold values from -0.15625 to 0.15625
- w_down: bfloat16 [6144, 1536], P('fsdp', ('dp', 'rows')), may hold values from -0.078125 to 0.078125
- layer_scale: float32 [1536], replicated, may hold values from 0.3 to 1.5
- d_out: bfloat16 [8, 16, 32, 1536], P(('dp', 'fsdp'), 'rows'), may hold values from -20 to 20
Outputs:
- result: bfloat16 [8, 16, 32, 1536], P(('dp', 'fsdp'), 'rows')
- grad_x: bfloat16 [8, 16, 32, 1536], P(('dp', 'fsdp'), 'rows')
- grad_up: float32 [1536, 6144], P(('dp', 'rows'), 'fsdp')
- grad_down: float32 [6144, 1536], P('fsdp', ('dp', 'rows'))
- grad_kernel: float32 [7, 7, 1536], replicated
- grad_gain: float32 [1536], replicated
- grad_scale: float32 [1536], replicated
All inputs are finite; a program needn't handle non-finite values.
Results may differ from a plain program's by a relative error of at most 0.0075.
Values may be sent and summed in bfloat16 or wider, within the bound.
No kernel may reach another device: no remote copies, remote signals or barrier semaphores. Data moves between devices by JAX's collectives and lax.ppermute only.
A program may use at most 128 MiB of HBM per device.

v0:
```python
import math
import jax
import jax.numpy as jnp
from jax import lax
from jax.sharding import PartitionSpec as P

KS = 7
norm_eps = 1e-06
inv_root_two = 1.0 / math.sqrt(2.0)
inv_root_two_pi = 1.0 / math.sqrt(2.0 * math.pi)
contract_rows = (((0,), (0,)), ((), ()))
contract_cols = (((1,), (1,)), ((), ()))


def padded_2(x, sides, width):
    for axis, dim in sides:
        devices, length = (lax.axis_size(axis), x.shape[dim])
        up = [(i, (i + 1) % devices) for i in range(devices - 1)]
        down = [(j, i) for i, j in up]
        last = lax.slice_in_dim(x, length - width, length, axis=dim)
        leading = lax.slice_in_dim(x, 0, width, axis=dim)
        before = lax.ppermute(last, axis, up)
        after = lax.ppermute(leading, axis, down)
        x = jnp.concatenate([before, x, after], axis=dim)
    return x


def gelu_exact(values):
    return 0.5 * values * (1.0 + jax.scipy.special.erf(values * inv_root_two))


def gelu_slope(values):
    cdf_part = 0.5 * (1.0 + jax.scipy.special.erf(values * inv_root_two))
    return cdf_part + values * jnp.exp(-0.5 * values * values) * inv_root_two_pi


def reduce_down(down_part):
    return lax.psum_scatter(down_part, ("dp", "rows"), scatter_dimension=1, tiled=True)


def body(feature_maps, dw_kernel, norm_gain, w_up, w_down, layer_scale, d_out):
    scenes, strip, across, width = feature_maps.shape
    cells = scenes * strip * across
    rimmed = padded_2(feature_maps, (("rows", 1),), 3)
    padded = jnp.pad(rimmed.astype(jnp.float32), ((0, 0), (0, 0), (3, 3), (0, 0)))
    filtered = jnp.zeros(feature_maps.shape, jnp.float32)
    for row_off in range(KS):
        for col_off in range(KS):
            filtered = (
                filtered
                + padded[:, row_off : row_off + strip, col_off : col_off + across, :]
                * dw_kernel[row_off, col_off]
            )
    flat = filtered.reshape(cells, width)
    average = jnp.mean(flat, axis=-1, keepdims=True)
    center = flat - average
    variance = jnp.mean(center * center, axis=-1, keepdims=True)
    rstd = lax.rsqrt(variance + norm_eps)
    normed = center * rstd
    scaled = (normed * norm_gain).astype(jnp.bfloat16)
    gathered = lax.all_gather(scaled, "fsdp", axis=0, tiled=True)
    up_full = lax.all_gather(w_up, ("dp", "rows"), axis=0, tiled=True)
    down_full = lax.all_gather(w_down, ("dp", "rows"), axis=1, tiled=True)
    hidden = jnp.dot(gathered, up_full, preferred_element_type=jnp.float32)
    active = gelu_exact(hidden).astype(jnp.bfloat16)
    mlp_terms = jnp.dot(active, down_full, preferred_element_type=jnp.float32)
    branch = lax.psum_scatter(
        mlp_terms.astype(jnp.bfloat16), "fsdp", scatter_dimension=0, tiled=True
    ).astype(jnp.float32)
    resid = feature_maps.reshape(cells, width).astype(jnp.float32)
    result = (resid + layer_scale * branch).astype(jnp.bfloat16).reshape(feature_maps.shape)
    cotan = d_out.reshape(cells, width).astype(jnp.float32)
    scale_part = jnp.sum(cotan * branch, axis=0)
    back = (cotan * layer_scale).astype(jnp.bfloat16)
    back_all = lax.all_gather(back, "fsdp", axis=0, tiled=True)
    down_part = lax.dot_general(active, back_all, contract_rows, preferred_element_type=jnp.float32)
    slope_in = lax.dot_general(
        back_all, down_full, contract_cols, preferred_element_type=jnp.float32
    )
    hidden_grad = (slope_in * gelu_slope(hidden)).astype(jnp.bfloat16)
    up_part = lax.dot_general(
        gathered, hidden_grad, contract_rows, preferred_element_type=jnp.float32
    )
    norm_terms = lax.dot_general(
        hidden_grad, up_full, contract_cols, preferred_element_type=jnp.float32
    )
    norm_grad = lax.psum_scatter(norm_terms, "fsdp", scatter_dimension=0, tiled=True)
    grad_up = lax.psum_scatter(up_part, ("dp", "rows"), scatter_dimension=0, tiled=True)
    grad_down = reduce_down(down_part)
    gain_part = jnp.sum(norm_grad * normed, axis=0)
    scaled_grad = norm_grad * norm_gain
    conv_grad = rstd * (
        scaled_grad
        - jnp.mean(scaled_grad, axis=-1, keepdims=True)
        - normed * jnp.mean(scaled_grad * normed, axis=-1, keepdims=True)
    )
    conv_grad = conv_grad.reshape(feature_maps.shape)
    grad_rim = padded_2(conv_grad.astype(jnp.bfloat16), (("rows", 1),), 3).astype(conv_grad.dtype)
    grad_pad = jnp.pad(grad_rim, ((0, 0), (0, 0), (3, 3), (0, 0)))
    kernel_rows = []
    back_conv = jnp.zeros(feature_maps.shape, jnp.float32)
    for row_off in range(KS):
        for col_off in range(KS):
            window = padded[:, row_off : row_off + strip, col_off : col_off + across, :]
            kernel_rows.append(jnp.sum(window * conv_grad, axis=(0, 1, 2)))
            back_conv = (
                back_conv
                + grad_pad[
                    :, 6 - row_off : 6 - row_off + strip, 6 - col_off : 6 - col_off + across, :
                ]
                * dw_kernel[row_off, col_off]
            )
    kernel_part = jnp.stack(kernel_rows).reshape(KS, KS, width)
    grad_x = (d_out.astype(jnp.float32) + back_conv).astype(jnp.bfloat16)
    grad_kernel, grad_gain, grad_scale = lax.psum(
        (kernel_part, gain_part, scale_part), ("dp", "fsdp", "rows")
    )
    return (result, grad_x, grad_up, grad_down, grad_kernel, grad_gain, grad_scale)


def solution(mesh):
    return jax.shard_map(
        body,
        mesh=mesh,
        in_specs=(
            P(("dp", "fsdp"), "rows", None, None),
            P(),
            P(),
            P(("dp", "rows"), "fsdp"),
            P("fsdp", ("dp", "rows")),
            P(),
            P(("dp", "fsdp"), "rows", None, None),
        ),
        out_specs=(
            P(("dp", "fsdp"), "rows", None, None),
            P(("dp", "fsdp"), "rows", None, None),
            P(("dp", "rows"), "fsdp"),
            P("fsdp", ("dp", "rows")),
            P(),
            P(),
            P(),
        ),
        check_vma=False,
    )
```

profile of v0, /device:TPU:0, one launch (start us, length us, event | category | flops | bytes accessed | tf_op | source)
XLA Modules:
  0.0 797.9 jit_solution(10668589192870983978)
XLA Ops:
  7.2 0.7 all-gather.3.cloned.1.call-update
  8.0 0.7 all-gather.5.cloned.1.call-update
  8.7 1.1 fusion.105
  9.8 2.4 collective-permute-start
  12.2 1.3 collective-permute-start.1
  13.5 1.3 slice_reduce_fusion.46
  14.9 0.3 slice_reduce_fusion.48
  15.5 0.9 slice_reduce_fusion.47
  16.4 1.4 collective-permute-done.1
  17.8 0.1 maximum_convert_fusion
  18.0 9.5 %fusion.103 = (f32[4,32]{1,0:T(4,128)S(1)}, f32[1,4,32,1536]{3,2,1,0:T(8,128)S(1)}) fusion(f32[1536]{0:T(1024)S(1)} %get-tuple-element.106, f32[1536]{0:T(1024)S(1)} %get-tuple-element.107, f32[1536]{0:T(1024)S(1)} %get-tuple-element.60, f32[1536]{0:T(1024)S(1)} %get-tuple-element.61, f32[1,10,32,1536]{3,2,1,0:T(8,128)S(1)} %maximum_convert_fusion, ...), kind=kLoop, calls=%fused_computation.314 | loop fusion | flops 19267456 | bytes 8641024 | tf_op jit(solution)/shard_map/reduce_sum | solution.py:55
  27.8 0.6 div.15
  28.4 0.2 multiply_reduce_fusion.51
  28.6 0.6 rsqrt.12
  29.3 0.8 multiply_convert_fusion.1
  30.1 8.6 %all_gather.12 = bf16[256,1536]{1,0:T(8,128)(2,1)} all-gather(bf16[128,1536]{1,0:T(8,128)(2,1)S(1)} %multiply_convert_fusion.1), channel_id=1, replica_groups=mesh['dp'=4,'fsdp'=2,'rows'=4] {'fsdp'}, dimensions={0}, use_global_device_ids=true | all-gather | bytes 1179648 | tf_op jit(solution)/shard_map/all_gather | solution.py:61
  38.7 55.8 %all-gather.3.cloned.1.call-done = bf16[1536,3072]{1,0:T(8,128)(2,1)} async-done(((bf16[96,3072]{1,0:T(8,128)(2,1)}), bf16[1536,3072]{1,0:T(8,128)(2,1)}) %all-gather.3.cloned.1.call-update) | async-done | bytes 9437200 | tf_op jit(solution)/shard_map/all_gather | solution.py:62
  94.5 8.2 %fusion.106 = f32[256,3072]{1,0:T(8,128)} fusion(bf16[256,1536]{1,0:T(8,128)(2,1)} %all_gather.12, bf16[1536,3072]{1,0:T(8,128)(2,1)} %all-gather.3.cloned.1.call-done), kind=kOutput, calls=%fused_computation.317 | convolution fusion | flops 2415919104 | bytes 13369344 | tf_op jit(solution)/shard_map/dot_general | solution.py:64
  102.7 73.7 %all-gather.5.cloned.1.call-done = bf16[3072,1536]{0,1:T(8,128)(2,1)} async-done(((bf16[3072,96]{0,1:T(8,128)(2,1)}), bf16[3072,1536]{0,1:T(8,128)(2,1)}) %all-gather.5.cloned.1.call-update) | async-done | bytes 9437200 | tf_op jit(solution)/shard_map/all_gather | solution.py:63
  176.4 8.2 %convolution_convert_fusion = bf16[256,1536]{1,0:T(8,128)(2,1)} fusion(bf16[3072,1536]{0,1:T(8,128)(2,1)} %all-gather.5.cloned.1.call-done, f32[256,3072]{1,0:T(8,128)} %fusion.106), kind=kOutput, calls=%fused_computation.93 | convolution fusion | flops 2420244480 | bytes 13369344 | tf_op jit(solution)/shard_map/dot_general | solution.py:66
  184.6 15.7 %reduce-scatter.5.cloned.1.call-done = bf16[128,1536]{1,0:T(8,128)(2,1)} async-done(((bf16[256,1536]{1,0:T(8,128)(2,1)}), bf16[128,1536]{1,0:T(8,128)(2,1)}) %reduce-scatter.5.cloned.1.call-update) | async-done | bytes 393232 | tf_op jit(solution)/shard_map/reduce_scatter | solution.py:67
  200.3 2.7 fusion.7
  203.0 11.8 %all_gather.15 = bf16[256,1536]{1,0:T(8,128)(2,1)S(1)} all-gather(bf16[128,1536]{1,0:T(8,128)(2,1)S(1)} %get-tuple-element.114), channel_id=1, replica_groups=mesh['dp'=4,'fsdp'=2,'rows'=4] {'fsdp'}, dimensions={0}, use_global_device_ids=true | all-gather | bytes 1179648 | tf_op jit(solution)/shard_map/all_gather | solution.py:75
  214.8 0.9 copy-done.2
  215.7 5.5 fusion
  221.3 1.2 copy-done.7
  222.5 3.8 fusion.107
  226.4 26.2 %reduce-scatter.7.cloned.1.call-done = f32[128,1536]{1,0:T(8,128)} async-done(((f32[256,1536]{1,0:T(8,128)}), f32[128,1536]{1,0:T(8,128)}) %reduce-scatter.7.cloned.1.call-update) | async-done | bytes 786448 | tf_op jit(solution)/shard_map/reduce_scatter | solution.py:87
  252.6 2.0 multiply_reduce_fusion
  254.6 3.6 multiply_reduce_fusion.2
  258.2 1.2 multiply_reduce_fusion.3
  259.4 2.0 multiply_reduce_fusion.1
  262.1 0.5 stack.199
  262.6 0.8 reshape.323
  263.5 11.1 %fusion.102 = f32[3072,1536]{0,1:T(8,128)} fusion(bf16[256,1536]{1,0:T(8,128)(2,1)S(1)} %copy-done.3, f32[256,3072]{1,0:T(8,128)} %fusion.106), kind=kOutput, calls=%fused_computation.313 | convolution fusion | flops 2419851264 | bytes 22806528 | tf_op jit(solution)/shard_map/dot_general | solution.py:76
  274.6 0.3 reduce-scatter.9.cloned.1.call-start
  274.9 0.8 copy-done.1
  275.7 0.5 copy-done.8
  276.2 7.9 fusion.108
  284.7 1.9 collective-permute-start.2
  286.5 1.3 collective-permute-start.3
  287.9 42.3 %all-reduce.2 = (f32[1536]{0:T(1024)}, f32[1536]{0:T(1024)}) all-reduce(f32[1536]{0:T(1024)} %get-tuple-element.56, f32[1536]{0:T(1024)} %get-tuple-element.113), channel_id=1, replica_groups=mesh['dp'=4,'fsdp'=2,'rows'=4] {'dp','fsdp','rows'}, use_global_device_ids=true, to_apply=%region_59.60 | all-reduce | flops 3072 | bytes 24576 | tf_op jit(solution)/shard_map/psum | solution.py:115
  330.2 0.1 maximum_convert_fusion.1
  330.7 7.5 fusion.95
  338.3 51.2 %all-reduce.5.cloned.1.call-done = f32[7,7,1536]{2,1,0:T(8,128)} async-done(((f32[7,7,1536]{2,1,0:T(8,128)}), f32[7,7,1536]{2,1,0:T(8,128)}) %all-reduce.5.cloned.1.call-update) | async-done | bytes 301072 | tf_op jit(solution)/shard_map/psum | solution.py:115
  389.4 200.8 %reduce-scatter.11.cloned.1.call-done = f32[3072,96]{0,1:T(8,128)} async-done(((f32[3072,1536]{0,1:T(8,128)}), f32[3072,96]{0,1:T(8,128)}) %reduce-scatter.11.cloned.1.call-update) | async-done | bytes 1179664 | tf_op jit(solution)/shard_map/reduce_scatter | solution.py:38
  590.2 199.1 %reduce-scatter.9.cloned.1.call-done = f32[96,3072]{1,0:T(8,128)} async-done(((f32[1536,3072]{1,0:T(8,128)}), f32[96,3072]{1,0:T(8,128)}) %reduce-scatter.9.cloned.1.call-update) | async-done | bytes 1179664 | tf_op jit(solution)/shard_map/reduce_scatter | solution.py:88
  789.3 1.7 copy.15
  (254 shorter events, 1.2 us)
Async XLA Ops:
  7.2 87.3 %all-gather.3.cloned.1.call-start = ((), (), s32[]{:S(2)}) async-start(), calls=%async_computation.4 | async-start | bytes 10027008 | tf_op jit(solution)/shard_map/all_gather | solution.py:62
  7.9 168.5 %all-gather.5.cloned.1.call-start = ((), (), s32[]{:S(2)}) async-start(), calls=%async_computation.5 | async-start | bytes 10027008 | tf_op jit(solution)/shard_map/all_gather | solution.py:63
  8.7 191.6 %reduce-scatter.5.cloned.1.call-start = ((), (), s32[]{:S(2)}) async-start(), calls=%async_computation.6 | async-start | bytes 1179648 | tf_op jit(solution)/shard_map/reduce_scatter | solution.py:67
  9.8 6.6 collective-permute-start
  12.2 5.6 collective-permute-start.1
  102.7 97.6 %copy-start.5 = (bf16[1,4,32,1536]{3,2,1,0:T(8,128)(2,1)S(1)}, bf16[1,4,32,1536]{3,2,1,0:T(8,128)(2,1)}, u32[]{:S(2)}) copy-start(bf16[1,4,32,1536]{3,2,1,0:T(8,128)(2,1)} %param.13) | copy-start | bytes 1179652
  184.6 68.0 %reduce-scatter.7.cloned.1.call-start = ((), (), s32[]{:S(2)}) async-start(), calls=%async_computation.7 | async-start | bytes 2359296 | tf_op jit(solution)/shard_map/reduce_scatter | solution.py:87
  226.3 163.1 %all-reduce.5.cloned.1.call-start = ((), (), s32[]{:S(2)}) async-start(), calls=%async_computation.10 | async-start | bytes 688128 | tf_op jit(solution)/shard_map/psum | solution.py:115
  263.4 326.7 %reduce-scatter.11.cloned.1.call-start = ((), (), s32[]{:S(2)}) async-start(), calls=%async_computation.9 | async-start | bytes 20054016 | tf_op jit(solution)/shard_map/reduce_scatter | solution.py:38
  274.6 514.7 %reduce-scatter.9.cloned.1.call-start = ((), (), s32[]{:S(2)}) async-start(), calls=%async_computation.8 | async-start | bytes 20054016 | tf_op jit(solution)/shard_map/reduce_scatter | solution.py:88
  284.2 46.1 %copy-start.6 = (bf16[1,4,32,1536]{3,2,1,0:T(8,128)(2,1)S(1)}, bf16[1,4,32,1536]{3,2,1,0:T(8,128)(2,1)}, u32[]{:S(2)}) copy-start(bf16[1,4,32,1536]{3,2,1,0:T(8,128)(2,1)} %param.13) | copy-start | bytes 1179652
  284.2 46.1 %copy-start.12 = (f32[1536]{0:T(1024)S(1)}, f32[1536]{0:T(1024)}, u32[]{:S(2)}) copy-start(f32[1536]{0:T(1024)} %copy-done.11) | copy-start | bytes 18436
  284.2 46.1 %copy-start.14 = (f32[1536]{0:T(1024)S(1)}, f32[1536]{0:T(1024)}, u32[]{:S(2)}) copy-start(f32[1536]{0:T(1024)} %copy-done.13) | copy-start | bytes 18436
  284.2 46.1 %copy-start.16 = (f32[1536]{0:T(1024)S(1)}, f32[1536]{0:T(1024)}, u32[]{:S(2)}) copy-start(f32[1536]{0:T(1024)} %copy-done.15) | copy-start | bytes 18436
  284.2 46.1 %copy-start.18 = (f32[1536]{0:T(1024)S(1)}, f32[1536]{0:T(1024)}, u32[]{:S(2)}) copy-start(f32[1536]{0:T(1024)} %copy-done.17) | copy-start | bytes 18436
  284.3 46.1 %copy-start.20 = (f32[1536]{0:T(1024)S(1)}, f32[1536]{0:T(1024)}, u32[]{:S(2)}) copy-start(f32[1536]{0:T(1024)} %copy-done.19) | copy-start | bytes 18436
  284.3 46.1 %copy-start.22 = (f32[1536]{0:T(1024)S(1)}, f32[1536]{0:T(1024)}, u32[]{:S(2)}) copy-start(f32[1536]{0:T(1024)} %copy-done.21) | copy-start | bytes 18436
  284.3 46.1 %copy-start.24 = (f32[1536]{0:T(1024)S(1)}, f32[1536]{0:T(1024)}, u32[]{:S(2)}) copy-start(f32[1536]{0:T(1024)} %copy-done.23) | copy-start | bytes 18436
  284.3 46.1 %copy-start.26 = (f32[1536]{0:T(1024)S(1)}, f32[1536]{0:T(1024)}, u32[]{:S(2)}) copy-start(f32[1536]{0:T(1024)} %copy-done.25) | copy-start | bytes 18436
  284.3 46.1 %copy-start.28 = (f32[1536]{0:T(1024)S(1)}, f32[1536]{0:T(1024)}, u32[]{:S(2)}) copy-start(f32[1536]{0:T(1024)} %copy-done.27) | copy-start | bytes 18436
  284.3 46.1 %copy-start.30 = (f32[1536]{0:T(1024)S(1)}, f32[1536]{0:T(1024)}, u32[]{:S(2)}) copy-start(f32[1536]{0:T(1024)} %copy-done.29) | copy-start | bytes 18436
  284.3 46.1 %copy-start.32 = (f32[1536]{0:T(1024)S(1)}, f32[1536]{0:T(1024)}, u32[]{:S(2)}) copy-start(f32[1536]{0:T(1024)} %copy-done.31) | copy-start | bytes 18436
  284.3 46.1 %copy-start.34 = (f32[1536]{0:T(1024)S(1)}, f32[1536]{0:T(1024)}, u32[]{:S(2)}) copy-start(f32[1536]{0:T(1024)} %copy-done.33) | copy-start | bytes 18436
  284.3 46.1 %copy-start.36 = (f32[1536]{0:T(1024)S(1)}, f32[1536]{0:T(1024)}, u32[]{:S(2)}) copy-start(f32[1536]{0:T(1024)} %copy-done.35) | copy-start | bytes 18436
  284.3 46.1 %copy-start.38 = (f32[1536]{0:T(1024)S(1)}, f32[1536]{0:T(1024)}, u32[]{:S(2)}) copy-start(f32[1536]{0:T(1024)} %copy-done.37) | copy-start | bytes 18436
  284.4 46.1 %copy-start.40 = (f32[1536]{0:T(1024)S(1)}, f32[1536]{0:T(1024)}, u32[]{:S(2)}) copy-start(f32[1536]{0:T(1024)} %copy-done.39) | copy-start | bytes 18436
  284.4 46.1 %copy-start.42 = (f32[1536]{0:T(1024)S(1)}, f32[1536]{0:T(1024)}, u32[]{:S(2)}) copy-start(f32[1536]{0:T(1024)} %copy-done.41) | copy-start | bytes 18436
  284.4 46.1 %copy-start.44 = (f32[1536]{0:T(1024)S(1)}, f32[1536]{0:T(1024)}, u32[]{:S(2)}) copy-start(f32[1536]{0:T(1024)} %copy-done.43) | copy-start | bytes 18436
  284.4 46.1 %copy-start.46 = (f32[1536]{0:T(1024)S(1)}, f32[1536]{0:T(1024)}, u32[]{:S(2)}) copy-start(f32[1536]{0:T(1024)} %copy-done.45) | copy-start | bytes 18436
  284.4 46.1 %copy-start.48 = (f32[1536]{0:T(1024)S(1)}, f32[1536]{0:T(1024)}, u32[]{:S(2)}) copy-start(f32[1536]{0:T(1024)} %copy-done.47) | copy-start | bytes 18436
  284.4 46.1 %copy-start.50 = (f32[1536]{0:T(1024)S(1)}, f32[1536]{0:T(1024)}, u32[]{:S(2)}) copy-start(f32[1536]{0:T(1024)} %copy-done.49) | copy-start | bytes 18436
  284.4 46.1 %copy-start.52 = (f32[1536]{0:T(1024)S(1)}, f32[1536]{0:T(1024)}, u32[]{:S(2)}) copy-start(f32[1536]{0:T(1024)} %copy-done.51) | copy-start | bytes 18436
  284.4 46.1 %copy-start.54 = (f32[1536]{0:T(1024)S(1)}, f32[1536]{0:T(1024)}, u32[]{:S(2)}) copy-start(f32[1536]{0:T(1024)} %copy-done.53) | copy-start | bytes 18436
  284.4 46.1 %copy-start.56 = (f32[1536]{0:T(1024)S(1)}, f32[1536]{0:T(1024)}, u32[]{:S(2)}) copy-start(f32[1536]{0:T(1024)} %copy-done.55) | copy-start | bytes 18436
  284.4 46.1 %copy-start.58 = (f32[1536]{0:T(1024)S(1)}, f32[1536]{0:T(1024)}, u32[]{:S(2)}) copy-start(f32[1536]{0:T(1024)} %copy-done.57) | copy-start | bytes 18436
  284.5 46.1 %copy-start.60 = (f32[1536]{0:T(1024)S(1)}, f32[1536]{0:T(1024)}, u32[]{:S(2)}) copy-start(f32[1536]{0:T(1024)} %copy-done.59) | copy-start | bytes 18436
  284.5 46.1 %copy-start.62 = (f32[1536]{0:T(1024)S(1)}, f32[1536]{0:T(1024)}, u32[]{:S(2)}) copy-start(f32[1536]{0:T(1024)} %copy-done.61) | copy-start | bytes 18436
  284.5 46.1 %copy-start.64 = (f32[1536]{0:T(1024)S(1)}, f32[1536]{0:T(1024)}, u32[]{:S(2)}) copy-start(f32[1536]{0:T(1024)} %copy-done.63) | copy-start | bytes 18436
  284.5 46.1 %copy-start.66 = (f32[1536]{0:T(1024)S(1)}, f32[1536]{0:T(1024)}, u32[]{:S(2)}) copy-start(f32[1536]{0:T(1024)} %copy-done.65) | copy-start | bytes 18436
  284.5 46.1 %copy-start.68 = (f32[1536]{0:T(1024)S(1)}, f32[1536]{0:T(1024)}, u32[]{:S(2)}) copy-start(f32[1536]{0:T(1024)} %copy-done.67) | copy-start | bytes 18436
  284.5 46.1 %copy-start.70 = (f32[1536]{0:T(1024)S(1)}, f32[1536]{0:T(1024)}, u32[]{:S(2)}) copy-start(f32[1536]{0:T(1024)} %copy-done.69) | copy-start | bytes 18436
  284.5 46.1 %copy-start.72 = (f32[1536]{0:T(1024)S(1)}, f32[1536]{0:T(1024)}, u32[]{:S(2)}) copy-start(f32[1536]{0:T(1024)} %copy-done.71) | copy-start | bytes 18436
  284.5 46.1 %copy-start.74 = (f32[1536]{0:T(1024)S(1)}, f32[1536]{0:T(1024)}, u32[]{:S(2)}) copy-start(f32[1536]{0:T(1024)} %copy-done.73) | copy-start | bytes 18436
  284.5 46.1 %copy-start.76 = (f32[1536]{0:T(1024)S(1)}, f32[1536]{0:T(1024)}, u32[]{:S(2)}) copy-start(f32[1536]{0:T(1024)} %copy-done.75) | copy-start | bytes 18436
  284.5 46.1 %copy-start.78 = (f32[1536]{0:T(1024)S(1)}, f32[1536]{0:T(1024)}, u32[]{:S(2)}) copy-start(f32[1536]{0:T(1024)} %copy-done.77) | copy-start | bytes 18436
  284.6 46.1 %copy-start.80 = (f32[1536]{0:T(1024)S(1)}, f32[1536]{0:T(1024)}, u32[]{:S(2)}) copy-start(f32[1536]{0:T(1024)} %copy-done.79) | copy-start | bytes 18436
  284.7 45.5 %collective-permute-start.2 = (bf16[1,3,32,1536]{3,2,1,0:T(8,128)(2,1)S(1)}, bf16[1,3,32,1536]{3,2,1,0:T(8,128)(2,1)S(1)}, u32[]{:S(2)}, u32[]{:S(2)}) collective-permute-start(bf16[1,3,32,1536]{3,2,1,0:T(8,128)(2,1)S(1)} %get-tuple-element.116), channel_id=1, source_target_pairs={{0,1},{1,2},{2,3},{4,5},{5,6},{6,7},{8,9},{9,10},{10,11},{12,13},{... | collective-permute-start | bytes 884744 | tf_op jit(solution)/shard_map/ppermute | solution.py:22
  286.5 43.6 %collective-permute-start.3 = (bf16[1,3,32,1536]{3,2,1,0:T(8,128)(2,1)S(1)}, bf16[1,3,32,1536]{3,2,1,0:T(8,128)(2,1)S(1)}, u32[]{:S(2)}, u32[]{:S(2)}) collective-permute-start(bf16[1,3,32,1536]{3,2,1,0:T(8,128)(2,1)S(1)} %get-tuple-element.117), channel_id=1, source_target_pairs={{1,0},{2,1},{3,2},{5,4},{6,5},{7,6},{9,8},{10,9},{11,10},{13,12},{... | collective-permute-start | bytes 884744 | tf_op jit(solution)/shard_map/ppermute | solution.py:23
  (57 other events, 803.9 us)
Sparse Core Ops, SparseCore 0:
  10.3 84.1 all-gather.2
  96.8 79.5 all-gather.4
  184.7 15.5 reduce-scatter.4
  226.4 26.0 reduce-scatter.6
  263.6 125.8 all-reduce.4
  394.5 195.6 reduce-scatter.10
  595.4 193.8 reduce-scatter.8
where the time goes:
time: 799 us; the launch traced here: 798 us
  waiting for transfers between devices  625 us (78%)
  blocking collectives  62.7 us (8%)
  matrix products  44.7 us (6%)
  other arithmetic  30 us (4%)
  between operations  16 us (2%)
  local copies, waits for them, and re-layouts  12.1 us (2%)
    reduce_scatter x1, waiting for transfers between devices, reduce_down(): lax.psum_scatter(down_part, ('dp', 'rows'), scatter_dimension=1, tiled=True)  201 us
    reduce_scatter x1, waiting for transfers between devices, body(): lax.psum_scatter(up_part, ('dp', 'rows'), scatter_dimension=0, tiled=True)  199 us
    all_gather x1, waiting for transfers between devices, body(): down_full = lax.all_gather(w_down, ('dp', 'rows'), axis=1, tiled=True)  73.7 us
    all_gather x1, waiting for transfers between devices, body(): up_full = lax.all_gather(w_up, ('dp', 'rows'), axis=0, tiled=True)  55.8 us
    psum x1, waiting for transfers between devices, body(): lax.psum((kernel_part, gain_part, scale_part), ('dp', 'fsdp', 'rows'))  51.2 us
    psum x1, blocking collectives, body(): lax.psum((kernel_part, gain_part, scale_part), ('dp', 'fsdp', 'rows'))  42.3 us
    reduce_scatter x1, waiting for transfers between devices, body(): lax.psum_scatter(norm_terms, 'fsdp', scatter_dimension=0, tiled=True)  26.2 us
  transfers between devices with their start and end apart: 11, of which 8 were waited for; matrix products, arithmetic and copies ran while one was open for 6% of the time, Pallas kernels for 0%

commit v1 on v0

--- a/solution.py
+++ b/solution.py
@@ -60,7 +60,22 @@
     scaled = (normed * norm_gain).astype(jnp.bfloat16)
     gathered = lax.all_gather(scaled, "fsdp", axis=0, tiled=True)
     up_full = lax.all_gather(w_up, ("dp", "rows"), axis=0, tiled=True)
-    down_full = lax.all_gather(w_down, ("dp", "rows"), axis=1, tiled=True)
+    ways, here, step = (
+        lax.axis_size(("dp", "rows")),
+        lax.axis_index(("dp", "rows")),
+        w_down.shape[1],
+    )
+    line, have = (w_down, 1)
+    while have < ways:
+        line = jnp.concatenate(
+            [
+                line,
+                lax.ppermute(line, ("dp", "rows"), [(d, (d - have) % ways) for d in range(ways)]),
+            ],
+            axis=1,
+        )
+        have = 2 * have
+    down_full = jnp.roll(line, here * step, axis=1)
     hidden = jnp.dot(gathered, up_full, preferred_element_type=jnp.float32)
     active = gelu_exact(hidden).astype(jnp.bfloat16)
     mlp_terms = jnp.dot(active, down_full, preferred_element_type=jnp.float32)

time: 799 us -> 1040 us (1.30)
  waiting for transfers between devices: 625 us -> 811 us
  local copies, waits for them, and re-layouts: 12.1 us -> 60.1 us
  starting transfers between devices: 7.34 us -> 19.5 us
    ppermute x0 -> x4, waiting for transfers between devices: none -> 312 us  [body(): lax.ppermute(line, ('dp', 'rows'), [(d, (d - have) % ways) for d in range...]
    all_gather x1 -> x0, waiting for transfers between devices: 73.7 us -> none  [body(): down_full = lax.all_gather(w_down, ('dp', 'rows'), axis=1, tiled=True)]
    all_gather x1, waiting for transfers between devices: 55.8 us -> 0.01 us  [body(): up_full = lax.all_gather(w_up, ('dp', 'rows'), axis=0, tiled=True)]
    another operation x50, local copies, waits for them, and re-layouts: 0.83 us -> 31 us  [body(): kernel_part = jnp.stack(kernel_rows).reshape(KS, KS, width)]
    unnamed x189 -> x222, local copies, waits for them, and re-layouts: 5.56 us -> 21.8 us
  transfers between devices with their start and end apart: 11 -> 14, of which waited for: 8 -> 9; matrix products, arithmetic and copies ran while one was open for 6% -> 6% of each run, Pallas kernels for 0% -> 0%
where the time goes in v1:
time: 1040 us
  waiting for transfers between devices  811 us (78%)
  blocking collectives  61 us (6%)
  local copies, waits for them, and re-layouts  60.1 us (6%)
  matrix products  42.4 us (4%)
  other arithmetic  33.4 us (3%)
  starting transfers between devices  19.5 us (2%)
  between operations  15.7 us (2%)
    ppermute x4, waiting for transfers between devices, body(): lax.ppermute(line, ('dp', 'rows'), [(d, (d - have) % ways) for d in range...  312 us
    reduce_scatter x1, waiting for transfers between devices, body(): lax.psum_scatter(up_part, ('dp', 'rows'), scatter_dimension=0, tiled=True)  201 us
    reduce_scatter x1, waiting for transfers between devices, reduce_down(): lax.psum_scatter(down_part, ('dp', 'rows'), scatter_dimension=1, tiled=True)  199 us
    psum x1, waiting for transfers between devices, body(): lax.psum((kernel_part, gain_part, scale_part), ('dp', 'fsdp', 'rows'))  52.9 us
    psum x1, blocking collectives, body(): lax.psum((kernel_part, gain_part, scale_part), ('dp', 'fsdp', 'rows'))  39.8 us
    another operation x50, local copies, waits for them, and re-layouts, body(): kernel_part = jnp.stack(kernel_rows).reshape(KS, KS, width)  31 us
    reduce_scatter x1, waiting for transfers between devices, body(): lax.psum_scatter(norm_terms, 'fsdp', scatter_dimension=0, tiled=True)  26.2 us
    unnamed x222, local copies, waits for them, and re-layouts  21.8 us
  transfers between devices with their start and end apart: 14, of which 9 were waited for; matrix products, arithmetic and copies ran while one was open for 6% of the time, Pallas kernels for 0%

profile of v1, /device:TPU:0, one launch (start us, length us, event | category | flops | bytes accessed | tf_op | source)
XLA Modules:
  0.0 1043.0 jit_solution(13965752553437972903)
XLA Ops:
  8.0 5.5 collective-permute-start.2
  13.5 7.7 collective-permute-done.2
  21.2 1.4 pad_maximum_fusion.2
  23.1 41.9 %collective-permute-done.3 = bf16[3072,192]{0,1:T(8,128)(2,1)S(1)} collective-permute-done((bf16[3072,192]{0,1:T(8,128)(2,1)S(1)}, bf16[3072,192]{0,1:T(8,128)(2,1)S(1)}, u32[]{:S(2)}, u32[]{:S(2)}) %collective-permute-start.3) | collective-permute-done | bytes 1179680 | tf_op jit(solution)/shard_map/ppermute | solution.py:73
  65.3 3.0 collective-permute-start.4
  68.2 89.5 %collective-permute-done.4 = bf16[3072,384]{0,1:T(8,128)(2,1)S(1)} collective-permute-done((bf16[3072,384]{0,1:T(8,128)(2,1)S(1)}, bf16[3072,384]{0,1:T(8,128)(2,1)S(1)}, u32[]{:S(2)}, u32[]{:S(2)}) %collective-permute-start.4) | collective-permute-done | bytes 2359328 | tf_op jit(solution)/shard_map/ppermute | solution.py:73
  157.8 2.5 pad_maximum_fusion
  160.7 1.1 collective-permute-start.5
  161.8 1.3 collective-permute-start.1
  163.1 3.0 collective-permute-start
  167.0 0.9 slice_reduce_fusion.47
  168.0 0.8 constant_dynamic-update-slice_fusion.9
  169.0 9.5 fusion.117
  179.5 9.6 all_gather.9
  189.1 1.9 constant_dynamic-update-slice_fusion.8
  191.0 1.1 constant_dynamic-update-slice_fusion.7
  192.1 1.5 constant_dynamic-update-slice_fusion.6
  193.7 173.3 %collective-permute-done.5 = bf16[3072,768]{0,1:T(8,128)(2,1)} collective-permute-done((bf16[3072,768]{0,1:T(8,128)(2,1)}, bf16[3072,768]{0,1:T(8,128)(2,1)}, u32[]{:S(2)}, u32[]{:S(2)}) %collective-permute-start.5) | collective-permute-done | bytes 4718624 | tf_op jit(solution)/shard_map/ppermute | solution.py:73
  367.0 4.8 constant_dynamic-update-slice_fusion.5
  373.5 1.1 constant_dynamic-update-slice_fusion.2
  374.6 1.7 constant_dynamic-update-slice_fusion.1
  376.3 4.9 constant_dynamic-update-slice_fusion
  381.1 5.3 fusion.120
  386.5 1.6 copy-done.13
  388.1 7.9 fusion.14
  396.3 18.8 %reduce-scatter.5.cloned.1.call-done = bf16[128,1536]{1,0:T(8,128)(2,1)} async-done(((bf16[256,1536]{1,0:T(8,128)(2,1)}), bf16[128,1536]{1,0:T(8,128)(2,1)}) %reduce-scatter.5.cloned.1.call-update) | async-done | bytes 393232 | tf_op jit(solution)/shard_map/reduce_scatter | solution.py:82
  415.0 2.7 fusion.19
  417.7 11.6 %all_gather.11 = bf16[256,1536]{1,0:T(8,128)(2,1)S(1)} all-gather(bf16[128,1536]{1,0:T(8,128)(2,1)S(1)} %get-tuple-element.114), channel_id=1, replica_groups=mesh['dp'=4,'fsdp'=2,'rows'=4] {'fsdp'}, dimensions={0}, use_global_device_ids=true | all-gather | bytes 1179648 | tf_op jit(solution)/shard_map/all_gather | solution.py:90
  429.4 0.9 copy-done.11
  430.3 6.4 fusion.7
  436.7 1.2 copy-done.17
  437.9 3.8 fusion.121
  441.8 26.2 %reduce-scatter.7.cloned.1.call-done = f32[128,1536]{1,0:T(8,128)} async-done(((f32[256,1536]{1,0:T(8,128)}), f32[128,1536]{1,0:T(8,128)}) %reduce-scatter.7.cloned.1.call-update) | async-done | bytes 786448 | tf_op jit(solution)/shard_map/reduce_scatter | solution.py:102
  468.0 2.0 multiply_reduce_fusion
  470.0 3.6 multiply_reduce_fusion.2
  473.6 1.2 multiply_reduce_fusion.3
  474.8 2.0 multiply_reduce_fusion.1
  502.0 5.9 stack.199
  508.8 8.0 fusion.122
  517.9 11.1 %fusion.116 = f32[3072,1536]{0,1:T(8,128)} fusion(bf16[256,1536]{1,0:T(8,128)(2,1)S(1)} %copy-done.12, f32[256,3072]{1,0:T(8,128)} %copy-done.13), kind=kOutput, calls=%fused_computation.332 | convolution fusion | flops 2419851264 | bytes 22806528 | tf_op jit(solution)/shard_map/dot_general | solution.py:91
  529.5 1.3 collective-permute-start.7
  530.8 3.0 collective-permute-start.6
  533.9 39.8 %all-reduce.2 = (f32[1536]{0:T(1024)}, f32[1536]{0:T(1024)}) all-reduce(f32[1536]{0:T(1024)} %get-tuple-element.56, f32[1536]{0:T(1024)} %get-tuple-element.113), channel_id=1, replica_groups=mesh['dp'=4,'fsdp'=2,'rows'=4] {'dp','fsdp','rows'}, use_global_device_ids=true, to_apply=%region_59.60 | all-reduce | flops 3072 | bytes 24576 | tf_op jit(solution)/shard_map/psum | solution.py:130
  574.2 7.5 fusion.107
  581.7 52.9 %all-reduce.5.cloned.1.call-done = f32[7,7,1536]{2,1,0:T(8,128)} async-done(((f32[7,7,1536]{2,1,0:T(8,128)}), f32[7,7,1536]{2,1,0:T(8,128)}) %all-reduce.5.cloned.1.call-update) | async-done | bytes 301072 | tf_op jit(solution)/shard_map/psum | solution.py:130
  634.6 200.8 %reduce-scatter.9.cloned.1.call-done = f32[96,3072]{1,0:T(8,128)} async-done(((f32[1536,3072]{1,0:T(8,128)}), f32[96,3072]{1,0:T(8,128)}) %reduce-scatter.9.cloned.1.call-update) | async-done | bytes 1179664 | tf_op jit(solution)/shard_map/reduce_scatter | solution.py:103
  835.4 199.0 %reduce-scatter.11.cloned.1.call-done = f32[3072,96]{0,1:T(8,128)} async-done(((f32[3072,1536]{0,1:T(8,128)}), f32[3072,96]{0,1:T(8,128)}) %reduce-scatter.11.cloned.1.call-update) | async-done | bytes 1179664 | tf_op jit(solution)/shard_map/reduce_scatter | solution.py:38
  1034.4 1.7 copy.24
  (296 shorter events, 32.9 us)
Async XLA Ops:
  7.2 57.9 %copy-start.4 = (bf16[3072,96]{0,1:T(8,128)(2,1)S(1)}, bf16[3072,96]{0,1:T(8,128)(2,1)}, u32[]{:S(2)}) copy-start(bf16[3072,96]{0,1:T(8,128)(2,1)} %param.11) | copy-start | bytes 1769476
  7.2 373.9 %all-gather.2.cloned.1.call-start = ((), (), s32[]{:S(2)}) async-start(), calls=%async_computation.4 | async-start | bytes 10027008 | tf_op jit(solution)/shard_map/all_gather | solution.py:62
  7.9 407.1 %reduce-scatter.5.cloned.1.call-start = ((), (), s32[]{:S(2)}) async-start(), calls=%async_computation.5 | async-start | bytes 1179648 | tf_op jit(solution)/shard_map/reduce_scatter | solution.py:82
  8.0 13.2 %collective-permute-start.2 = (bf16[3072,96]{0,1:T(8,128)(2,1)}, bf16[3072,96]{0,1:T(8,128)(2,1)S(1)}, u32[]{:S(2)}, u32[]{:S(2)}) collective-permute-start(bf16[3072,96]{0,1:T(8,128)(2,1)} %param.11), channel_id=1, source_target_pairs={{0,27},{1,0},{2,1},{3,2},{8,3},{9,8},{10,9},{11,10},{16,11},{17,16... | collective-permute-start | bytes 1769480 | tf_op jit(solution)/shard_map/ppermute | solution.py:73
  21.2 136.6 %copy-start.5 = (bf16[3072,96]{0,1:T(8,128)(2,1)}, bf16[3072,96]{0,1:T(8,128)(2,1)S(1)}, u32[]{:S(2)}) copy-start(bf16[3072,96]{0,1:T(8,128)(2,1)S(1)} %collective-permute-done.2) | copy-start | bytes 1769476
  22.6 42.5 %collective-permute-start.3 = (bf16[3072,192]{0,1:T(8,128)(2,1)S(1)}, bf16[3072,192]{0,1:T(8,128)(2,1)S(1)}, u32[]{:S(2)}, u32[]{:S(2)}) collective-permute-start(bf16[3072,192]{0,1:T(8,128)(2,1)S(1)} %pad_maximum_fusion.2), channel_id=1, source_target_pairs={{0,26},{1,27},{2,0},{3,1},{8,2},{9,3},{10,8},{11,9},{16,10},{17,11... | collective-permute-start | bytes 3538952 | tf_op jit(solution)/shard_map/ppermute | solution.py:73
  65.1 95.2 %copy-start.2 = (bf16[3072,192]{0,1:T(8,128)(2,1)}, bf16[3072,192]{0,1:T(8,128)(2,1)S(1)}, u32[]{:S(2)}) copy-start(bf16[3072,192]{0,1:T(8,128)(2,1)S(1)} %collective-permute-done.3) | copy-start | bytes 3538948
  65.2 96.5 %copy-start.7 = (bf16[1,4,32,1536]{3,2,1,0:T(8,128)(2,1)S(1)}, bf16[1,4,32,1536]{3,2,1,0:T(8,128)(2,1)}, u32[]{:S(2)}) copy-start(bf16[1,4,32,1536]{3,2,1,0:T(8,128)(2,1)} %param.7) | copy-start | bytes 1179652
  65.3 101.0 %copy-start.19 = (f32[7,7,1536]{2,1,0:T(8,128)S(1)}, f32[7,7,1536]{2,1,0:T(8,128)}, u32[]{:S(2)}) copy-start(f32[7,7,1536]{2,1,0:T(8,128)} %param.8) | copy-start | bytes 903172
  65.3 92.5 %collective-permute-start.4 = (bf16[3072,384]{0,1:T(8,128)(2,1)S(1)}, bf16[3072,384]{0,1:T(8,128)(2,1)S(1)}, u32[]{:S(2)}, u32[]{:S(2)}) collective-permute-start(bf16[3072,384]{0,1:T(8,128)(2,1)S(1)} %pad_maximum_fusion.1), channel_id=1, source_target_pairs={{0,24},{1,25},{2,26},{3,27},{8,0},{9,1},{10,2},{11,3},{16,8},{17,9... | collective-permute-start | bytes 7077896 | tf_op jit(solution)/shard_map/ppermute | solution.py:73
  160.7 206.3 %collective-permute-start.5 = (bf16[3072,768]{0,1:T(8,128)(2,1)}, bf16[3072,768]{0,1:T(8,128)(2,1)}, u32[]{:S(2)}, u32[]{:S(2)}) collective-permute-start(bf16[3072,768]{0,1:T(8,128)(2,1)} %pad_maximum_fusion), channel_id=1, source_target_pairs={{0,16},{1,17},{2,18},{3,19},{8,24},{9,25},{10,26},{11,27},{16,0},{... | collective-permute-start | bytes 14155784 | tf_op jit(solution)/shard_map/ppermute | solution.py:73
  161.8 7.0 collective-permute-start.1
  163.1 5.7 collective-permute-start
  193.7 179.0 %copy-start.6 = (bf16[3072,96]{0,1:T(8,128)(2,1)S(1)}, bf16[3072,96]{0,1:T(8,128)(2,1)}, u32[]{:S(2)}) copy-start(bf16[3072,96]{0,1:T(8,128)(2,1)} %copy-done.5) | copy-start | bytes 1769476
  396.0 71.9 %reduce-scatter.7.cloned.1.call-start = ((), (), s32[]{:S(2)}) async-start(), calls=%async_computation.6 | async-start | bytes 2359296 | tf_op jit(solution)/shard_map/reduce_scatter | solution.py:102
  441.7 192.9 %all-reduce.5.cloned.1.call-start = ((), (), s32[]{:S(2)}) async-start(), calls=%async_computation.9 | async-start | bytes 688128 | tf_op jit(solution)/shard_map/psum | solution.py:130
  508.7 326.6 %reduce-scatter.9.cloned.1.call-start = ((), (), s32[]{:S(2)}) async-start(), calls=%async_computation.7 | async-start | bytes 20054016 | tf_op jit(solution)/shard_map/reduce_scatter | solution.py:103
  516.8 517.6 %reduce-scatter.11.cloned.1.call-start = ((), (), s32[]{:S(2)}) async-start(), calls=%async_computation.8 | async-start | bytes 20054016 | tf_op jit(solution)/shard_map/reduce_scatter | solution.py:38
  529.0 44.8 %copy-start.16 = (bf16[1,4,32,1536]{3,2,1,0:T(8,128)(2,1)S(1)}, bf16[1,4,32,1536]{3,2,1,0:T(8,128)(2,1)}, u32[]{:S(2)}) copy-start(bf16[1,4,32,1536]{3,2,1,0:T(8,128)(2,1)} %param.13) | copy-start | bytes 1179652
  529.0 44.8 %copy-start.22 = (f32[1536]{0:T(1024)S(1)}, f32[1536]{0:T(1024)}, u32[]{:S(2)}) copy-start(f32[1536]{0:T(1024)} %copy-done.21) | copy-start | bytes 18436
  529.0 44.8 %copy-start.24 = (f32[1536]{0:T(1024)S(1)}, f32[1536]{0:T(1024)}, u32[]{:S(2)}) copy-start(f32[1536]{0:T(1024)} %copy-done.23) | copy-start | bytes 18436
  529.0 44.8 %copy-start.26 = (f32[1536]{0:T(1024)S(1)}, f32[1536]{0:T(1024)}, u32[]{:S(2)}) copy-start(f32[1536]{0:T(1024)} %copy-done.25) | copy-start | bytes 18436
  529.0 44.8 %copy-start.28 = (f32[1536]{0:T(1024)S(1)}, f32[1536]{0:T(1024)}, u32[]{:S(2)}) copy-start(f32[1536]{0:T(1024)} %copy-done.27) | copy-start | bytes 18436
  529.0 44.8 %copy-start.30 = (f32[1536]{0:T(1024)S(1)}, f32[1536]{0:T(1024)}, u32[]{:S(2)}) copy-start(f32[1536]{0:T(1024)} %copy-done.29) | copy-start | bytes 18436
  529.1 44.8 %copy-start.32 = (f32[1536]{0:T(1024)S(1)}, f32[1536]{0:T(1024)}, u32[]{:S(2)}) copy-start(f32[1536]{0:T(1024)} %copy-done.31) | copy-start | bytes 18436
  529.1 44.8 %copy-start.34 = (f32[1536]{0:T(1024)S(1)}, f32[1536]{0:T(1024)}, u32[]{:S(2)}) copy-start(f32[1536]{0:T(1024)} %copy-done.33) | copy-start | bytes 18436
  529.1 44.8 %copy-start.36 = (f32[1536]{0:T(1024)S(1)}, f32[1536]{0:T(1024)}, u32[]{:S(2)}) copy-start(f32[1536]{0:T(1024)} %copy-done.35) | copy-start | bytes 18436
  529.1 44.8 %copy-start.38 = (f32[1536]{0:T(1024)S(1)}, f32[1536]{0:T(1024)}, u32[]{:S(2)}) copy-start(f32[1536]{0:T(1024)} %copy-done.37) | copy-start | bytes 18436
  529.1 44.8 %copy-start.40 = (f32[1536]{0:T(1024)S(1)}, f32[1536]{0:T(1024)}, u32[]{:S(2)}) copy-start(f32[1536]{0:T(1024)} %copy-done.39) | copy-start | bytes 18436
  529.1 44.8 %copy-start.42 = (f32[1536]{0:T(1024)S(1)}, f32[1536]{0:T(1024)}, u32[]{:S(2)}) copy-start(f32[1536]{0:T(1024)} %copy-done.41) | copy-start | bytes 18436
  529.1 44.8 %copy-start.44 = (f32[1536]{0:T(1024)S(1)}, f32[1536]{0:T(1024)}, u32[]{:S(2)}) copy-start(f32[1536]{0:T(1024)} %copy-done.43) | copy-start | bytes 18436
  529.1 44.8 %copy-start.46 = (f32[1536]{0:T(1024)S(1)}, f32[1536]{0:T(1024)}, u32[]{:S(2)}) copy-start(f32[1536]{0:T(1024)} %copy-done.45) | copy-start | bytes 18436
  529.1 44.8 %copy-start.48 = (f32[1536]{0:T(1024)S(1)}, f32[1536]{0:T(1024)}, u32[]{:S(2)}) copy-start(f32[1536]{0:T(1024)} %copy-done.47) | copy-start | bytes 18436
  529.2 44.8 %copy-start.50 = (f32[1536]{0:T(1024)S(1)}, f32[1536]{0:T(1024)}, u32[]{:S(2)}) copy-start(f32[1536]{0:T(1024)} %copy-done.49) | copy-start | bytes 18436
  529.2 44.8 %copy-start.52 = (f32[1536]{0:T(1024)S(1)}, f32[1536]{0:T(1024)}, u32[]{:S(2)}) copy-start(f32[1536]{0:T(1024)} %copy-done.51) | copy-start | bytes 18436
  529.2 44.8 %copy-start.54 = (f32[1536]{0:T(1024)S(1)}, f32[1536]{0:T(1024)}, u32[]{:S(2)}) copy-start(f32[1536]{0:T(1024)} %copy-done.53) | copy-start | bytes 18436
  529.2 44.8 %copy-start.56 = (f32[1536]{0:T(1024)S(1)}, f32[1536]{0:T(1024)}, u32[]{:S(2)}) copy-start(f32[1536]{0:T(1024)} %copy-done.55) | copy-start | bytes 18436
  529.2 44.8 %copy-start.58 = (f32[1536]{0:T(1024)S(1)}, f32[1536]{0:T(1024)}, u32[]{:S(2)}) copy-start(f32[1536]{0:T(1024)} %copy-done.57) | copy-start | bytes 18436
  529.2 44.8 %copy-start.60 = (f32[1536]{0:T(1024)S(1)}, f32[1536]{0:T(1024)}, u32[]{:S(2)}) copy-start(f32[1536]{0:T(1024)} %copy-done.59) | copy-start | bytes 18436
  529.2 44.8 %copy-start.62 = (f32[1536]{0:T(1024)S(1)}, f32[1536]{0:T(1024)}, u32[]{:S(2)}) copy-start(f32[1536]{0:T(1024)} %copy-done.61) | copy-start | bytes 18436
  529.2 44.8 %copy-start.64 = (f32[1536]{0:T(1024)S(1)}, f32[1536]{0:T(1024)}, u32[]{:S(2)}) copy-start(f32[1536]{0:T(1024)} %copy-done.63) | copy-start | bytes 18436
  529.2 44.8 %copy-start.66 = (f32[1536]{0:T(1024)S(1)}, f32[1536]{0:T(1024)}, u32[]{:S(2)}) copy-start(f32[1536]{0:T(1024)} %copy-done.65) | copy-start | bytes 18436
  529.2 44.8 %copy-start.68 = (f32[1536]{0:T(1024)S(1)}, f32[1536]{0:T(1024)}, u32[]{:S(2)}) copy-start(f32[1536]{0:T(1024)} %copy-done.67) | copy-start | bytes 18436
  529.3 44.8 %copy-start.70 = (f32[1536]{0:T(1024)S(1)}, f32[1536]{0:T(1024)}, u32[]{:S(2)}) copy-start(f32[1536]{0:T(1024)} %copy-done.69) | copy-start | bytes 18436
  529.3 44.8 %copy-start.72 = (f32[1536]{0:T(1024)S(1)}, f32[1536]{0:T(1024)}, u32[]{:S(2)}) copy-start(f32[1536]{0:T(1024)} %copy-done.71) | copy-start | bytes 18436
  529.3 44.8 %copy-start.74 = (f32[1536]{0:T(1024)S(1)}, f32[1536]{0:T(1024)}, u32[]{:S(2)}) copy-start(f32[1536]{0:T(1024)} %copy-done.73) | copy-start | bytes 18436
  529.5 44.2 %collective-permute-start.7 = (bf16[1,3,32,1536]{3,2,1,0:T(8,128)(2,1)S(1)}, bf16[1,3,32,1536]{3,2,1,0:T(8,128)(2,1)S(1)}, u32[]{:S(2)}, u32[]{:S(2)}) collective-permute-start(bf16[1,3,32,1536]{3,2,1,0:T(8,128)(2,1)S(1)} %get-tuple-element.117), channel_id=1, source_target_pairs={{1,0},{2,1},{3,2},{5,4},{6,5},{7,6},{9,8},{10,9},{11,10},{13,12},{... | collective-permute-start | bytes 884744 | tf_op jit(solution)/shard_map/ppermute | solution.py:23
  530.8 42.9 %collective-permute-start.6 = (bf16[1,3,32,1536]{3,2,1,0:T(8,128)(2,1)S(1)}, bf16[1,3,32,1536]{3,2,1,0:T(8,128)(2,1)S(1)}, u32[]{:S(2)}, u32[]{:S(2)}) collective-permute-start(bf16[1,3,32,1536]{3,2,1,0:T(8,128)(2,1)S(1)} %get-tuple-element.116), channel_id=1, source_target_pairs={{0,1},{1,2},{2,3},{4,5},{5,6},{6,7},{8,9},{9,10},{10,11},{12,13},{... | collective-permute-start | bytes 884744 | tf_op jit(solution)/shard_map/ppermute | solution.py:22
  (72 other events, 1295.9 us)
Sparse Core Ops, SparseCore 0:
  10.3 138.0 all-gather.1
  396.1 18.8 reduce-scatter.4
  441.8 26.0 reduce-scatter.6
  508.9 125.6 all-reduce.4
  639.7 195.6 reduce-scatter.8
  840.5 193.8 reduce-scatter.10
